TPU v7x, 512 devices: a whole 4x8x8 slice. The times are simulated.
512 devices in a mesh: sep: 8 (over y), row: 8 (over z), col: 8 (over x, core).
Axes of the slice: x: 4, y: 8, z: 8, core: 2. Of those that a mesh axis runs over, the one named last changes fastest.
Arguments:
- right_sides: float32 [2, 16, 32768], P(None, None, ('sep', 'row', 'col')), may hold values from -6 to 6
- inverse_diag: float32 [8, 4096, 4096], P('sep', ('row', 'col')), may hold values from -0.09375 to 0.09375
- lower_blocks: float32 [8, 2048, 4096], P('sep', ('row', 'col')), may hold values from -0.09375 to 0.09375
- targets: int32 [8, 2048], P('sep', ('row', 'col')), may hold values from 0 to 32767, as said below
- counts: int32 [8, 64], P('sep', ('row', 'col')), may hold values from 0 to 32, as said below
Outputs:
- solution: float32 [2, 16, 32768], P(None, None, ('sep', 'row', 'col'))
Inputs may be any that keep to these rules, and one draw needn't show every extreme that they name: For every separator s and lower row j: targets[s, j] // 4096 > s, except for the last separator whose counts are all zero; and (targets[s, j] % 4096) // 64 == j // 32. The last separator's counts are zero; every other separator has a block with exactly 32 live rows, and the others at least one.
All inputs are finite; a program needn't handle non-finite values.
Results may differ from a plain program's by a relative error of at most 0.0001.
Values sent between devices are 32-bit elements; how exact they have to be, the bound alone decides.
No kernel may reach another device: no remote copies, remote signals or barrier semaphores. Data moves between devices by JAX's collectives and lax.ppermute only.
A program may use at most 64 MiB of HBM per device.

v0:
```python
import jax
import jax.numpy as jnp
from jax import lax
from jax.sharding import PartitionSpec as P


def passed_along(block, axis, distance):
    devices = range(lax.axis_size(axis))
    route = [(i - distance, i) for i in devices if i - distance in devices]
    return lax.ppermute(block, axis, route)


def shards(right_sides, inverse_diag, lower_blocks, targets, counts):
    levels = lax.axis_size("sep")
    own_level = lax.axis_index("sep")
    batches, width_rhs, own_rows = right_sides.shape
    width = inverse_diag.shape[-1]
    given = right_sides.reshape(batches * width_rhs, own_rows)
    diag_rows = inverse_diag[0]
    lower_rows = lower_blocks[0]
    lower_count = lower_rows.shape[0]
    live = jnp.arange(lower_count, dtype=jnp.int32) < counts[0, 0]
    places = targets[0] // width * own_rows + targets[0] % own_rows

    def solve_piece(segment):
        return lax.dot_general(
            segment,
            diag_rows,
            (((1,), (1,)), ((), ())),
            precision=lax.Precision.HIGHEST,
            preferred_element_type=jnp.float32,
        )

    def lower_piece(segment):
        return lax.dot_general(
            segment,
            lower_rows,
            (((1,), (1,)), ((), ())),
            precision=lax.Precision.HIGHEST,
            preferred_element_type=jnp.float32,
        )

    def one_level(level, state):
        carried, solution = state
        resid = given - lax.dynamic_slice_in_dim(carried, level * own_rows, own_rows, 1)
        solved = solve_piece(lax.all_gather(resid, ("row", "col"), axis=1, tiled=True))
        solution = jnp.where(own_level == level, solved, solution)
        update = lower_piece(lax.all_gather(solved, ("row", "col"), axis=1, tiled=True))
        update = jnp.where(live[None, :], update, jnp.float32(0.0))
        carried = carried.at[:, places].add(update)
        return (passed_along(carried, "sep", 1), solution)

    carried = jnp.zeros((given.shape[0], levels * own_rows), jnp.float32)
    solution = jnp.zeros_like(given)
    carried, solution = lax.fori_loop(0, levels - 1, one_level, (carried, solution))
    last = levels - 1
    resid = given - carried[:, last * own_rows :]
    solved = solve_piece(lax.all_gather(resid, ("row", "col"), axis=1, tiled=True))
    solution = jnp.where(own_level == last, solved, solution)
    return solution.reshape(batches, width_rhs, own_rows)


def solution(mesh):
    placed = (
        P(None, None, ("sep", "row", "col")),
        P("sep", ("row", "col"), None),
        P("sep", ("row", "col"), None),
        P("sep", ("row", "col")),
        P("sep", ("row", "col")),
    )
    return jax.shard_map(
        shards,
        mesh=mesh,
        in_specs=placed,
        out_specs=P(None, None, ("sep", "row", "col")),
        check_vma=False,
    )
```

profile of v0, /device:TPU:33, one launch (start us, length us, event | category | flops | bytes accessed | tf_op | source)
XLA Modules:
  0.0 871.5 jit_solution(13566988338382411557)
XLA Ops:
  1.5 816.8 %while.16 = (s32[]{:T(128)}, f32[32,512]{0,1:T(8,128)S(1)}, f32[32,64]{1,0:T(8,128)S(1)}, s32[32]{0:T(128)S(1)}, f32[32,64]{0,1:T(8,128)S(1)}, /*index=5*/f32[64...) while((s32[]{:T(128)}, f32[32,512]{0,1:T(8,128)S(1)}, ...), condition=%wide.region_2.3_spmd.clone, body=%wide.region_0.2_spmd.clone.sunk | while | flops 151003264 | bytes 14787303 | solution.py:55
  1.8 57.0 %all-gather.7 = f32[64,64,32]{1,2,0:T(8,128)S(1)} all-gather(f32[1,64,32]{1,2,0:T(8,128)S(1)} %subtract_bitcast_fusion.2), channel_id=1, replica_groups=mesh['sep'=8,'row'=8,'col'=8] {'row','col'}, dimensions={0}, use_global_device_ids=true | all-gather | bytes 532480 | tf_op jit(solution)/shard_map/while/body/eval_jaxpr/all_gather | solution.py:46
  61.6 49.6 %all-gather.8 = f32[64,64,32]{1,2,0:T(8,128)S(1)} all-gather(f32[1,64,32]{1,2,0:T(8,128)S(1)} %bitcast.68), channel_id=1, replica_groups=mesh['sep'=8,'row'=8,'col'=8] {'row','col'}, dimensions={0}, use_global_device_ids=true | all-gather | bytes 532480 | tf_op jit(solution)/shard_map/while/body/eval_jaxpr/all_gather | solution.py:48
  114.4 2.3 collective-permute-start
  116.7 8.5 collective-permute-done
  125.5 48.8 %all-gather.7 = f32[64,64,32]{1,2,0:T(8,128)S(1)} all-gather(f32[1,64,32]{1,2,0:T(8,128)S(1)} %subtract_bitcast_fusion.2), channel_id=1, replica_groups=mesh['sep'=8,'row'=8,'col'=8] {'row','col'}, dimensions={0}, use_global_device_ids=true | all-gather | bytes 532480 | tf_op jit(solution)/shard_map/while/body/eval_jaxpr/all_gather | solution.py:46
  177.1 49.6 %all-gather.8 = f32[64,64,32]{1,2,0:T(8,128)S(1)} all-gather(f32[1,64,32]{1,2,0:T(8,128)S(1)} %bitcast.68), channel_id=1, replica_groups=mesh['sep'=8,'row'=8,'col'=8] {'row','col'}, dimensions={0}, use_global_device_ids=true | all-gather | bytes 532480 | tf_op jit(solution)/shard_map/while/body/eval_jaxpr/all_gather | solution.py:48
  229.9 1.9 collective-permute-start
  231.8 8.9 %collective-permute-done = f32[32,512]{0,1:T(8,128)S(1)} collective-permute-done((f32[32,512]{0,1:T(8,128)S(1)}, f32[32,512]{0,1:T(8,128)S(1)}, u32[]{:S(2)}, u32[]{:S(2)}) %collective-permute-start) | collective-permute-done | bytes 65568 | tf_op jit(solution)/shard_map/while/body/eval_jaxpr/ppermute | solution.py:10
  241.0 48.8 %all-gather.7 = f32[64,64,32]{1,2,0:T(8,128)S(1)} all-gather(f32[1,64,32]{1,2,0:T(8,128)S(1)} %subtract_bitcast_fusion.2), channel_id=1, replica_groups=mesh['sep'=8,'row'=8,'col'=8] {'row','col'}, dimensions={0}, use_global_device_ids=true | all-gather | bytes 532480 | tf_op jit(solution)/shard_map/while/body/eval_jaxpr/all_gather | solution.py:46
  291.7 1.0 select_select_fusion.2
  292.6 49.6 %all-gather.8 = f32[64,64,32]{1,2,0:T(8,128)S(1)} all-gather(f32[1,64,32]{1,2,0:T(8,128)S(1)} %bitcast.68), channel_id=1, replica_groups=mesh['sep'=8,'row'=8,'col'=8] {'row','col'}, dimensions={0}, use_global_device_ids=true | all-gather | bytes 532480 | tf_op jit(solution)/shard_map/while/body/eval_jaxpr/all_gather | solution.py:48
  345.4 1.9 collective-permute-start
  347.3 8.9 %collective-permute-done = f32[32,512]{0,1:T(8,128)S(1)} collective-permute-done((f32[32,512]{0,1:T(8,128)S(1)}, f32[32,512]{0,1:T(8,128)S(1)}, u32[]{:S(2)}, u32[]{:S(2)}) %collective-permute-start) | collective-permute-done | bytes 65568 | tf_op jit(solution)/shard_map/while/body/eval_jaxpr/ppermute | solution.py:10
  356.5 48.8 %all-gather.7 = f32[64,64,32]{1,2,0:T(8,128)S(1)} all-gather(f32[1,64,32]{1,2,0:T(8,128)S(1)} %subtract_bitcast_fusion.2), channel_id=1, replica_groups=mesh['sep'=8,'row'=8,'col'=8] {'row','col'}, dimensions={0}, use_global_device_ids=true | all-gather | bytes 532480 | tf_op jit(solution)/shard_map/while/body/eval_jaxpr/all_gather | solution.py:46
  408.2 49.6 %all-gather.8 = f32[64,64,32]{1,2,0:T(8,128)S(1)} all-gather(f32[1,64,32]{1,2,0:T(8,128)S(1)} %bitcast.68), channel_id=1, replica_groups=mesh['sep'=8,'row'=8,'col'=8] {'row','col'}, dimensions={0}, use_global_device_ids=true | all-gather | bytes 532480 | tf_op jit(solution)/shard_map/while/body/eval_jaxpr/all_gather | solution.py:48
  460.9 1.9 collective-permute-start
  462.9 8.9 %collective-permute-done = f32[32,512]{0,1:T(8,128)S(1)} collective-permute-done((f32[32,512]{0,1:T(8,128)S(1)}, f32[32,512]{0,1:T(8,128)S(1)}, u32[]{:S(2)}, u32[]{:S(2)}) %collective-permute-start) | collective-permute-done | bytes 65568 | tf_op jit(solution)/shard_map/while/body/eval_jaxpr/ppermute | solution.py:10
  472.0 48.8 %all-gather.7 = f32[64,64,32]{1,2,0:T(8,128)S(1)} all-gather(f32[1,64,32]{1,2,0:T(8,128)S(1)} %subtract_bitcast_fusion.2), channel_id=1, replica_groups=mesh['sep'=8,'row'=8,'col'=8] {'row','col'}, dimensions={0}, use_global_device_ids=true | all-gather | bytes 532480 | tf_op jit(solution)/shard_map/while/body/eval_jaxpr/all_gather | solution.py:46
  523.7 49.6 %all-gather.8 = f32[64,64,32]{1,2,0:T(8,128)S(1)} all-gather(f32[1,64,32]{1,2,0:T(8,128)S(1)} %bitcast.68), channel_id=1, replica_groups=mesh['sep'=8,'row'=8,'col'=8] {'row','col'}, dimensions={0}, use_global_device_ids=true | all-gather | bytes 532480 | tf_op jit(solution)/shard_map/while/body/eval_jaxpr/all_gather | solution.py:48
  576.4 1.9 collective-permute-start
  578.4 8.9 %collective-permute-done = f32[32,512]{0,1:T(8,128)S(1)} collective-permute-done((f32[32,512]{0,1:T(8,128)S(1)}, f32[32,512]{0,1:T(8,128)S(1)}, u32[]{:S(2)}, u32[]{:S(2)}) %collective-permute-start) | collective-permute-done | bytes 65568 | tf_op jit(solution)/shard_map/while/body/eval_jaxpr/ppermute | solution.py:10
  587.6 48.8 %all-gather.7 = f32[64,64,32]{1,2,0:T(8,128)S(1)} all-gather(f32[1,64,32]{1,2,0:T(8,128)S(1)} %subtract_bitcast_fusion.2), channel_id=1, replica_groups=mesh['sep'=8,'row'=8,'col'=8] {'row','col'}, dimensions={0}, use_global_device_ids=true | all-gather | bytes 532480 | tf_op jit(solution)/shard_map/while/body/eval_jaxpr/all_gather | solution.py:46
  639.2 49.6 %all-gather.8 = f32[64,64,32]{1,2,0:T(8,128)S(1)} all-gather(f32[1,64,32]{1,2,0:T(8,128)S(1)} %bitcast.68), channel_id=1, replica_groups=mesh['sep'=8,'row'=8,'col'=8] {'row','col'}, dimensions={0}, use_global_device_ids=true | all-gather | bytes 532480 | tf_op jit(solution)/shard_map/while/body/eval_jaxpr/all_gather | solution.py:48
  692.0 1.9 collective-permute-start
  693.9 8.9 %collective-permute-done = f32[32,512]{0,1:T(8,128)S(1)} collective-permute-done((f32[32,512]{0,1:T(8,128)S(1)}, f32[32,512]{0,1:T(8,128)S(1)}, u32[]{:S(2)}, u32[]{:S(2)}) %collective-permute-start) | collective-permute-done | bytes 65568 | tf_op jit(solution)/shard_map/while/body/eval_jaxpr/ppermute | solution.py:10
  703.1 48.8 %all-gather.7 = f32[64,64,32]{1,2,0:T(8,128)S(1)} all-gather(f32[1,64,32]{1,2,0:T(8,128)S(1)} %subtract_bitcast_fusion.2), channel_id=1, replica_groups=mesh['sep'=8,'row'=8,'col'=8] {'row','col'}, dimensions={0}, use_global_device_ids=true | all-gather | bytes 532480 | tf_op jit(solution)/shard_map/while/body/eval_jaxpr/all_gather | solution.py:46
  754.7 49.6 %all-gather.8 = f32[64,64,32]{1,2,0:T(8,128)S(1)} all-gather(f32[1,64,32]{1,2,0:T(8,128)S(1)} %bitcast.68), channel_id=1, replica_groups=mesh['sep'=8,'row'=8,'col'=8] {'row','col'}, dimensions={0}, use_global_device_ids=true | all-gather | bytes 532480 | tf_op jit(solution)/shard_map/while/body/eval_jaxpr/all_gather | solution.py:48
  807.5 1.9 collective-permute-start
  809.4 8.9 %collective-permute-done = f32[32,512]{0,1:T(8,128)S(1)} collective-permute-done((f32[32,512]{0,1:T(8,128)S(1)}, f32[32,512]{0,1:T(8,128)S(1)}, u32[]{:S(2)}, u32[]{:S(2)}) %collective-permute-start) | collective-permute-done | bytes 65568 | tf_op jit(solution)/shard_map/while/body/eval_jaxpr/ppermute | solution.py:10
  819.1 49.0 %all-gather.2 = f32[64,64,32]{1,2,0:T(8,128)S(1)} all-gather(f32[1,64,32]{1,2,0:T(8,128)S(1)} %fusion.4), channel_id=1, replica_groups=mesh['sep'=8,'row'=8,'col'=8] {'row','col'}, dimensions={0}, use_global_device_ids=true | all-gather | bytes 532480 | tf_op jit(solution)/shard_map/all_gather | solution.py:58
  870.0 1.6 convolution_select_fusion.1
  (139 shorter events, 46.4 us)
Async XLA Ops:
  0.8 0.7 copy-start.4
  59.4 1.2 copy-start
  111.8 1.0 copy-start.2
  114.4 10.8 %collective-permute-start = (f32[32,512]{0,1:T(8,128)S(1)}, f32[32,512]{0,1:T(8,128)S(1)}, u32[]{:S(2)}, u32[]{:S(2)}) collective-permute-start(f32[32,512]{0,1:T(8,128)S(1)} %scatter_fusion), channel_id=1, source_target_pairs={{0,64},{64,128},{128,192},{192,256},{256,320},{320,384},{384,448},... | collective-permute-start | bytes 196616 | tf_op jit(solution)/shard_map/while/body/eval_jaxpr/ppermute | solution.py:10
  174.9 1.2 copy-start
  227.4 1.0 copy-start.2
  229.9 10.8 %collective-permute-start = (f32[32,512]{0,1:T(8,128)S(1)}, f32[32,512]{0,1:T(8,128)S(1)}, u32[]{:S(2)}, u32[]{:S(2)}) collective-permute-start(f32[32,512]{0,1:T(8,128)S(1)} %scatter_fusion), channel_id=1, source_target_pairs={{0,64},{64,128},{128,192},{192,256},{256,320},{320,384},{384,448},... | collective-permute-start | bytes 196616 | tf_op jit(solution)/shard_map/while/body/eval_jaxpr/ppermute | solution.py:10
  290.5 1.2 copy-start
  342.9 1.0 copy-start.2
  345.4 10.8 %collective-permute-start = (f32[32,512]{0,1:T(8,128)S(1)}, f32[32,512]{0,1:T(8,128)S(1)}, u32[]{:S(2)}, u32[]{:S(2)}) collective-permute-start(f32[32,512]{0,1:T(8,128)S(1)} %scatter_fusion), channel_id=1, source_target_pairs={{0,64},{64,128},{128,192},{192,256},{256,320},{320,384},{384,448},... | collective-permute-start | bytes 196616 | tf_op jit(solution)/shard_map/while/body/eval_jaxpr/ppermute | solution.py:10
  406.0 1.2 copy-start
  458.4 1.0 copy-start.2
  460.9 10.8 %collective-permute-start = (f32[32,512]{0,1:T(8,128)S(1)}, f32[32,512]{0,1:T(8,128)S(1)}, u32[]{:S(2)}, u32[]{:S(2)}) collective-permute-start(f32[32,512]{0,1:T(8,128)S(1)} %scatter_fusion), channel_id=1, source_target_pairs={{0,64},{64,128},{128,192},{192,256},{256,320},{320,384},{384,448},... | collective-permute-start | bytes 196616 | tf_op jit(solution)/shard_map/while/body/eval_jaxpr/ppermute | solution.py:10
  521.5 1.2 copy-start
  573.9 1.0 copy-start.2
  576.4 10.8 %collective-permute-start = (f32[32,512]{0,1:T(8,128)S(1)}, f32[32,512]{0,1:T(8,128)S(1)}, u32[]{:S(2)}, u32[]{:S(2)}) collective-permute-start(f32[32,512]{0,1:T(8,128)S(1)} %scatter_fusion), channel_id=1, source_target_pairs={{0,64},{64,128},{128,192},{192,256},{256,320},{320,384},{384,448},... | collective-permute-start | bytes 196616 | tf_op jit(solution)/shard_map/while/body/eval_jaxpr/ppermute | solution.py:10
  637.0 1.2 copy-start
  689.4 1.0 copy-start.2
  692.0 10.8 %collective-permute-start = (f32[32,512]{0,1:T(8,128)S(1)}, f32[32,512]{0,1:T(8,128)S(1)}, u32[]{:S(2)}, u32[]{:S(2)}) collective-permute-start(f32[32,512]{0,1:T(8,128)S(1)} %scatter_fusion), channel_id=1, source_target_pairs={{0,64},{64,128},{128,192},{192,256},{256,320},{320,384},{384,448},... | collective-permute-start | bytes 196616 | tf_op jit(solution)/shard_map/while/body/eval_jaxpr/ppermute | solution.py:10
  752.5 1.2 copy-start
  804.9 1.0 copy-start.2
  807.5 10.8 %collective-permute-start = (f32[32,512]{0,1:T(8,128)S(1)}, f32[32,512]{0,1:T(8,128)S(1)}, u32[]{:S(2)}, u32[]{:S(2)}) collective-permute-start(f32[32,512]{0,1:T(8,128)S(1)} %scatter_fusion), channel_id=1, source_target_pairs={{0,64},{64,128},{128,192},{192,256},{256,320},{320,384},{384,448},... | collective-permute-start | bytes 196616 | tf_op jit(solution)/shard_map/while/body/eval_jaxpr/ppermute | solution.py:10
  818.3 0.7 copy-start.3
  868.7 1.2 copy-start.1
where the time goes:
time: 873 us; the launch traced here: 872 us
  blocking collectives  746 us (85%)
  waiting for transfers between devices  61.8 us (7%)
  local copies, waits for them, and re-layouts  25.6 us (3%)
  starting transfers between devices  13.8 us (2%)
  matrix products  12.1 us (1%)
  other arithmetic  11.3 us (1%)
    all_gather x7, blocking collectives, one_level(): lax.all_gather(resid, ('row', 'col'), axis=1, tiled=True)  350 us
    all_gather x7, blocking collectives, one_level(): lax.all_gather(solved, ('row', 'col'), axis=1, tiled=True)  347 us
    ppermute x7, waiting for transfers between devices, passed_along(): return lax.ppermute(block, axis, route)  61.8 us
    all_gather x1, blocking collectives, shards(): lax.all_gather(resid, ('row', 'col'), axis=1, tiled=True)  49 us
  transfers between devices with their start and end apart: 7, of which 7 were waited for; matrix products, arithmetic and copies ran while one was open for 0% of the time, Pallas kernels for 0%

commit v1 on v0

--- a/solution.py
+++ b/solution.py
@@ -45,7 +45,14 @@
         resid = given - lax.dynamic_slice_in_dim(carried, level * own_rows, own_rows, 1)
         solved = solve_piece(lax.all_gather(resid, ("row", "col"), axis=1, tiled=True))
         solution = jnp.where(own_level == level, solved, solution)
-        update = lower_piece(lax.all_gather(solved, ("row", "col"), axis=1, tiled=True))
+        update = lower_piece(
+            jnp.concatenate(
+                lax.all_to_all(
+                    jnp.stack([solved] * lax.axis_size(("row", "col"))), ("row", "col"), 0, 0
+                ),
+                axis=1,
+            )
+        )
         update = jnp.where(live[None, :], update, jnp.float32(0.0))
         carried = carried.at[:, places].add(update)
         return (passed_along(carried, "sep", 1), solution)

time: 873 us -> 727 us (0.83)
  blocking collectives: 746 us -> 409 us
  waiting for transfers between devices: 61.8 us -> 179 us
  starting transfers between devices: 13.8 us -> 52.1 us
  local copies, waits for them, and re-layouts: 25.6 us -> 47.7 us
  other arithmetic: 11.3 us -> 24.3 us
    all_gather x7 -> x0, blocking collectives: 347 us -> none  [one_level(): lax.all_gather(solved, ('row', 'col'), axis=1, tiled=True)]
    all_to_all x0 -> x7, waiting for transfers between devices: none -> 119 us  [one_level(): lax.all_to_all(jnp.stack([solved] * lax.axis_size(('row', 'col'))), ('row...]
    all_to_all x0 -> x7, starting transfers between devices: none -> 38.2 us  [one_level(): lax.all_to_all(jnp.stack([solved] * lax.axis_size(('row', 'col'))), ('row...]
    while x63 -> x70, local copies, waits for them, and re-layouts: 12.5 us -> 27.6 us
    all_to_all x0 -> x7, other arithmetic: none -> 13 us  [one_level(): lax.all_to_all(jnp.stack([solved] * lax.axis_size(('row', 'col'))), ('row...]
  transfers between devices with their start and end apart: 7 -> 14, of which waited for: 7 -> 14; matrix products, arithmetic and copies ran while one was open for 0% -> 1% of each run, Pallas kernels for 0% -> 0%
where the time goes in v1:
time: 727 us; the launch traced here: 725 us
  blocking collectives  409 us (56%)
  waiting for transfers between devices  179 us (25%)
  starting transfers between devices  52.1 us (7%)
  local copies, waits for them, and re-layouts  47.7 us (7%)
  other arithmetic  24.3 us (3%)
  matrix products  12.1 us (2%)
    all_gather x7, blocking collectives, one_level(): lax.all_gather(resid, ('row', 'col'), axis=1, tiled=True)  358 us
    all_to_all x7, waiting for transfers between devices, one_level(): lax.all_to_all(jnp.stack([solved] * lax.axis_size(('row', 'col'))), ('row...  119 us
    ppermute x7, waiting for transfers between devices, passed_along(): return lax.ppermute(block, axis, route)  60.1 us
    all_gather x1, blocking collectives, shards(): lax.all_gather(resid, ('row', 'col'), axis=1, tiled=True)  50.4 us
    all_to_all x7, starting transfers between devices, one_level(): lax.all_to_all(jnp.stack([solved] * lax.axis_size(('row', 'col'))), ('row...  38.2 us
    while x70, local copies, waits for them, and re-layouts  27.6 us
  transfers between devices with their start and end apart: 14, of which 14 were waited for; matrix products, arithmetic and copies ran while one was open for 1% of the time, Pallas kernels for 0%

profile of v1, /device:TPU:33, one launch (start us, length us, event | category | flops | bytes accessed | tf_op | source)
XLA Modules:
  0.0 725.3 jit_solution(15725340925829995400)
XLA Ops:
  1.5 669.2 %while.16 = (s32[]{:T(128)}, f32[32,512]{0,1:T(8,128)S(1)}, f32[32,64]{1,0:T(8,128)S(1)}, s32[32]{0:T(128)S(1)}, f32[32,64]{0,1:T(8,128)S(1)}, /*index=5*/f32[64...) while((s32[]{:T(128)}, f32[32,512]{0,1:T(8,128)S(1)}, ...), condition=%wide.region_2.3_spmd.clone, body=%wide.region_0.2_spmd.clone.sunk | while | flops 151003264 | bytes 19505948 | solution.py:62
  1.8 57.0 %all-gather.4 = f32[64,64,32]{1,2,0:T(8,128)S(1)} all-gather(f32[1,64,32]{1,2,0:T(8,128)S(1)} %subtract_bitcast_fusion.2), channel_id=1, replica_groups=mesh['sep'=8,'row'=8,'col'=8] {'row','col'}, dimensions={0}, use_global_device_ids=true | all-gather | bytes 532480 | tf_op jit(solution)/shard_map/while/body/eval_jaxpr/all_gather | solution.py:46
  63.2 5.6 all-to-all-start
  69.4 17.0 %all-to-all-done = f32[64,1,2048]{2,1,0:T(1,128)S(1)} async-done(((f32[64,1,2048]{2,1,0:T(1,128)}), f32[64,1,2048]{2,1,0:T(1,128)S(1)}, u32[]{:S(2)}, u32[]{:S(2)}) %all-to-all-start) | async-done | bytes 524320 | tf_op jit(solution)/shard_map/while/body/eval_jaxpr/all_to_all | solution.py:50
  92.4 2.3 collective-permute-start
  94.7 8.3 %collective-permute-done = f32[32,512]{0,1:T(8,128)S(1)} collective-permute-done((f32[32,512]{0,1:T(8,128)S(1)}, f32[32,512]{0,1:T(8,128)S(1)}, u32[]{:S(2)}, u32[]{:S(2)}) %collective-permute-start) | collective-permute-done | bytes 65568 | tf_op jit(solution)/shard_map/while/body/eval_jaxpr/ppermute | solution.py:10
  103.3 50.2 %all-gather.4 = f32[64,64,32]{1,2,0:T(8,128)S(1)} all-gather(f32[1,64,32]{1,2,0:T(8,128)S(1)} %subtract_bitcast_fusion.2), channel_id=1, replica_groups=mesh['sep'=8,'row'=8,'col'=8] {'row','col'}, dimensions={0}, use_global_device_ids=true | all-gather | bytes 532480 | tf_op jit(solution)/shard_map/while/body/eval_jaxpr/all_gather | solution.py:46
  157.9 5.4 all-to-all-start
  164.0 17.0 %all-to-all-done = f32[64,1,2048]{2,1,0:T(1,128)S(1)} async-done(((f32[64,1,2048]{2,1,0:T(1,128)}), f32[64,1,2048]{2,1,0:T(1,128)S(1)}, u32[]{:S(2)}, u32[]{:S(2)}) %all-to-all-start) | async-done | bytes 524320 | tf_op jit(solution)/shard_map/while/body/eval_jaxpr/all_to_all | solution.py:50
  189.0 8.6 %collective-permute-done = f32[32,512]{0,1:T(8,128)S(1)} collective-permute-done((f32[32,512]{0,1:T(8,128)S(1)}, f32[32,512]{0,1:T(8,128)S(1)}, u32[]{:S(2)}, u32[]{:S(2)}) %collective-permute-start) | collective-permute-done | bytes 65568 | tf_op jit(solution)/shard_map/while/body/eval_jaxpr/ppermute | solution.py:10
  197.9 50.2 %all-gather.4 = f32[64,64,32]{1,2,0:T(8,128)S(1)} all-gather(f32[1,64,32]{1,2,0:T(8,128)S(1)} %subtract_bitcast_fusion.2), channel_id=1, replica_groups=mesh['sep'=8,'row'=8,'col'=8] {'row','col'}, dimensions={0}, use_global_device_ids=true | all-gather | bytes 532480 | tf_op jit(solution)/shard_map/while/body/eval_jaxpr/all_gather | solution.py:46
  252.5 5.4 all-to-all-start
  258.7 17.0 %all-to-all-done = f32[64,1,2048]{2,1,0:T(1,128)S(1)} async-done(((f32[64,1,2048]{2,1,0:T(1,128)}), f32[64,1,2048]{2,1,0:T(1,128)S(1)}, u32[]{:S(2)}, u32[]{:S(2)}) %all-to-all-start) | async-done | bytes 524320 | tf_op jit(solution)/shard_map/while/body/eval_jaxpr/all_to_all | solution.py:50
  281.6 1.9 collective-permute-start
  283.6 8.6 %collective-permute-done = f32[32,512]{0,1:T(8,128)S(1)} collective-permute-done((f32[32,512]{0,1:T(8,128)S(1)}, f32[32,512]{0,1:T(8,128)S(1)}, u32[]{:S(2)}, u32[]{:S(2)}) %collective-permute-start) | collective-permute-done | bytes 65568 | tf_op jit(solution)/shard_map/while/body/eval_jaxpr/ppermute | solution.py:10
  292.5 50.2 %all-gather.4 = f32[64,64,32]{1,2,0:T(8,128)S(1)} all-gather(f32[1,64,32]{1,2,0:T(8,128)S(1)} %subtract_bitcast_fusion.2), channel_id=1, replica_groups=mesh['sep'=8,'row'=8,'col'=8] {'row','col'}, dimensions={0}, use_global_device_ids=true | all-gather | bytes 532480 | tf_op jit(solution)/shard_map/while/body/eval_jaxpr/all_gather | solution.py:46
  347.1 5.4 all-to-all-start
  353.3 17.0 %all-to-all-done = f32[64,1,2048]{2,1,0:T(1,128)S(1)} async-done(((f32[64,1,2048]{2,1,0:T(1,128)}), f32[64,1,2048]{2,1,0:T(1,128)S(1)}, u32[]{:S(2)}, u32[]{:S(2)}) %all-to-all-start) | async-done | bytes 524320 | tf_op jit(solution)/shard_map/while/body/eval_jaxpr/all_to_all | solution.py:50
  378.2 8.6 %collective-permute-done = f32[32,512]{0,1:T(8,128)S(1)} collective-permute-done((f32[32,512]{0,1:T(8,128)S(1)}, f32[32,512]{0,1:T(8,128)S(1)}, u32[]{:S(2)}, u32[]{:S(2)}) %collective-permute-start) | collective-permute-done | bytes 65568 | tf_op jit(solution)/shard_map/while/body/eval_jaxpr/ppermute | solution.py:10
  387.1 50.2 %all-gather.4 = f32[64,64,32]{1,2,0:T(8,128)S(1)} all-gather(f32[1,64,32]{1,2,0:T(8,128)S(1)} %subtract_bitcast_fusion.2), channel_id=1, replica_groups=mesh['sep'=8,'row'=8,'col'=8] {'row','col'}, dimensions={0}, use_global_device_ids=true | all-gather | bytes 532480 | tf_op jit(solution)/shard_map/while/body/eval_jaxpr/all_gather | solution.py:46
  441.7 5.4 all-to-all-start
  447.9 17.0 %all-to-all-done = f32[64,1,2048]{2,1,0:T(1,128)S(1)} async-done(((f32[64,1,2048]{2,1,0:T(1,128)}), f32[64,1,2048]{2,1,0:T(1,128)S(1)}, u32[]{:S(2)}, u32[]{:S(2)}) %all-to-all-start) | async-done | bytes 524320 | tf_op jit(solution)/shard_map/while/body/eval_jaxpr/all_to_all | solution.py:50
  472.8 8.6 %collective-permute-done = f32[32,512]{0,1:T(8,128)S(1)} collective-permute-done((f32[32,512]{0,1:T(8,128)S(1)}, f32[32,512]{0,1:T(8,128)S(1)}, u32[]{:S(2)}, u32[]{:S(2)}) %collective-permute-start) | collective-permute-done | bytes 65568 | tf_op jit(solution)/shard_map/while/body/eval_jaxpr/ppermute | solution.py:10
  481.7 50.2 %all-gather.4 = f32[64,64,32]{1,2,0:T(8,128)S(1)} all-gather(f32[1,64,32]{1,2,0:T(8,128)S(1)} %subtract_bitcast_fusion.2), channel_id=1, replica_groups=mesh['sep'=8,'row'=8,'col'=8] {'row','col'}, dimensions={0}, use_global_device_ids=true | all-gather | bytes 532480 | tf_op jit(solution)/shard_map/while/body/eval_jaxpr/all_gather | solution.py:46
  536.4 5.4 all-to-all-start
  542.5 17.0 %all-to-all-done = f32[64,1,2048]{2,1,0:T(1,128)S(1)} async-done(((f32[64,1,2048]{2,1,0:T(1,128)}), f32[64,1,2048]{2,1,0:T(1,128)S(1)}, u32[]{:S(2)}, u32[]{:S(2)}) %all-to-all-start) | async-done | bytes 524320 | tf_op jit(solution)/shard_map/while/body/eval_jaxpr/all_to_all | solution.py:50
  567.4 8.6 %collective-permute-done = f32[32,512]{0,1:T(8,128)S(1)} collective-permute-done((f32[32,512]{0,1:T(8,128)S(1)}, f32[32,512]{0,1:T(8,128)S(1)}, u32[]{:S(2)}, u32[]{:S(2)}) %collective-permute-start) | collective-permute-done | bytes 65568 | tf_op jit(solution)/shard_map/while/body/eval_jaxpr/ppermute | solution.py:10
  576.3 50.2 %all-gather.4 = f32[64,64,32]{1,2,0:T(8,128)S(1)} all-gather(f32[1,64,32]{1,2,0:T(8,128)S(1)} %subtract_bitcast_fusion.2), channel_id=1, replica_groups=mesh['sep'=8,'row'=8,'col'=8] {'row','col'}, dimensions={0}, use_global_device_ids=true | all-gather | bytes 532480 | tf_op jit(solution)/shard_map/while/body/eval_jaxpr/all_gather | solution.py:46
  631.0 5.4 all-to-all-start
  637.1 17.0 %all-to-all-done = f32[64,1,2048]{2,1,0:T(1,128)S(1)} async-done(((f32[64,1,2048]{2,1,0:T(1,128)}), f32[64,1,2048]{2,1,0:T(1,128)S(1)}, u32[]{:S(2)}, u32[]{:S(2)}) %all-to-all-start) | async-done | bytes 524320 | tf_op jit(solution)/shard_map/while/body/eval_jaxpr/all_to_all | solution.py:50
  662.0 8.6 %collective-permute-done = f32[32,512]{0,1:T(8,128)S(1)} collective-permute-done((f32[32,512]{0,1:T(8,128)S(1)}, f32[32,512]{0,1:T(8,128)S(1)}, u32[]{:S(2)}, u32[]{:S(2)}) %collective-permute-start) | collective-permute-done | bytes 65568 | tf_op jit(solution)/shard_map/while/body/eval_jaxpr/ppermute | solution.py:10
  671.5 50.4 %all-gather.1 = f32[64,64,32]{1,2,0:T(8,128)S(1)} all-gather(f32[1,64,32]{1,2,0:T(8,128)S(1)} %fusion.4), channel_id=1, replica_groups=mesh['sep'=8,'row'=8,'col'=8] {'row','col'}, dimensions={0}, use_global_device_ids=true | all-gather | bytes 532480 | tf_op jit(solution)/shard_map/all_gather | solution.py:65
  (181 shorter events, 93.7 us)
Async XLA Ops:
  0.8 0.7 copy-start.4
  59.4 1.2 copy-start
  63.2 23.3 %all-to-all-start = ((f32[64,1,2048]{2,1,0:T(1,128)}), f32[64,1,2048]{2,1,0:T(1,128)S(1)}, u32[]{:S(2)}, u32[]{:S(2)}) async-start(f32[64,1,2048]{2,1,0:T(1,128)} %reshape.73), calls=%async_computation | async-start | bytes 1048576 | tf_op jit(solution)/shard_map/while/body/eval_jaxpr/all_to_all | solution.py:50
  89.9 1.0 copy-start.2
  92.4 10.6 %collective-permute-start = (f32[32,512]{0,1:T(8,128)S(1)}, f32[32,512]{0,1:T(8,128)S(1)}, u32[]{:S(2)}, u32[]{:S(2)}) collective-permute-start(f32[32,512]{0,1:T(8,128)S(1)} %scatter_fusion), channel_id=1, source_target_pairs={{0,64},{64,128},{128,192},{192,256},{256,320},{320,384},{384,448},... | collective-permute-start | bytes 196616 | tf_op jit(solution)/shard_map/while/body/eval_jaxpr/ppermute | solution.py:10
  154.1 1.2 copy-start
  157.9 23.1 %all-to-all-start = ((f32[64,1,2048]{2,1,0:T(1,128)}), f32[64,1,2048]{2,1,0:T(1,128)S(1)}, u32[]{:S(2)}, u32[]{:S(2)}) async-start(f32[64,1,2048]{2,1,0:T(1,128)} %reshape.73), calls=%async_computation | async-start | bytes 1048576 | tf_op jit(solution)/shard_map/while/body/eval_jaxpr/all_to_all | solution.py:50
  184.5 1.0 copy-start.2
  187.0 10.6 %collective-permute-start = (f32[32,512]{0,1:T(8,128)S(1)}, f32[32,512]{0,1:T(8,128)S(1)}, u32[]{:S(2)}, u32[]{:S(2)}) collective-permute-start(f32[32,512]{0,1:T(8,128)S(1)} %scatter_fusion), channel_id=1, source_target_pairs={{0,64},{64,128},{128,192},{192,256},{256,320},{320,384},{384,448},... | collective-permute-start | bytes 196616 | tf_op jit(solution)/shard_map/while/body/eval_jaxpr/ppermute | solution.py:10
  248.8 1.2 copy-start
  252.5 23.1 %all-to-all-start = ((f32[64,1,2048]{2,1,0:T(1,128)}), f32[64,1,2048]{2,1,0:T(1,128)S(1)}, u32[]{:S(2)}, u32[]{:S(2)}) async-start(f32[64,1,2048]{2,1,0:T(1,128)} %reshape.73), calls=%async_computation | async-start | bytes 1048576 | tf_op jit(solution)/shard_map/while/body/eval_jaxpr/all_to_all | solution.py:50
  279.1 1.0 copy-start.2
  281.6 10.6 %collective-permute-start = (f32[32,512]{0,1:T(8,128)S(1)}, f32[32,512]{0,1:T(8,128)S(1)}, u32[]{:S(2)}, u32[]{:S(2)}) collective-permute-start(f32[32,512]{0,1:T(8,128)S(1)} %scatter_fusion), channel_id=1, source_target_pairs={{0,64},{64,128},{128,192},{192,256},{256,320},{320,384},{384,448},... | collective-permute-start | bytes 196616 | tf_op jit(solution)/shard_map/while/body/eval_jaxpr/ppermute | solution.py:10
  343.4 1.2 copy-start
  347.1 23.1 %all-to-all-start = ((f32[64,1,2048]{2,1,0:T(1,128)}), f32[64,1,2048]{2,1,0:T(1,128)S(1)}, u32[]{:S(2)}, u32[]{:S(2)}) async-start(f32[64,1,2048]{2,1,0:T(1,128)} %reshape.73), calls=%async_computation | async-start | bytes 1048576 | tf_op jit(solution)/shard_map/while/body/eval_jaxpr/all_to_all | solution.py:50
  373.7 1.0 copy-start.2
  376.2 10.6 %collective-permute-start = (f32[32,512]{0,1:T(8,128)S(1)}, f32[32,512]{0,1:T(8,128)S(1)}, u32[]{:S(2)}, u32[]{:S(2)}) collective-permute-start(f32[32,512]{0,1:T(8,128)S(1)} %scatter_fusion), channel_id=1, source_target_pairs={{0,64},{64,128},{128,192},{192,256},{256,320},{320,384},{384,448},... | collective-permute-start | bytes 196616 | tf_op jit(solution)/shard_map/while/body/eval_jaxpr/ppermute | solution.py:10
  438.0 1.2 copy-start
  441.7 23.1 %all-to-all-start = ((f32[64,1,2048]{2,1,0:T(1,128)}), f32[64,1,2048]{2,1,0:T(1,128)S(1)}, u32[]{:S(2)}, u32[]{:S(2)}) async-start(f32[64,1,2048]{2,1,0:T(1,128)} %reshape.73), calls=%async_computation | async-start | bytes 1048576 | tf_op jit(solution)/shard_map/while/body/eval_jaxpr/all_to_all | solution.py:50
  468.3 1.0 copy-start.2
  470.9 10.6 %collective-permute-start = (f32[32,512]{0,1:T(8,128)S(1)}, f32[32,512]{0,1:T(8,128)S(1)}, u32[]{:S(2)}, u32[]{:S(2)}) collective-permute-start(f32[32,512]{0,1:T(8,128)S(1)} %scatter_fusion), channel_id=1, source_target_pairs={{0,64},{64,128},{128,192},{192,256},{256,320},{320,384},{384,448},... | collective-permute-start | bytes 196616 | tf_op jit(solution)/shard_map/while/body/eval_jaxpr/ppermute | solution.py:10
  532.6 1.2 copy-start
  536.4 23.1 %all-to-all-start = ((f32[64,1,2048]{2,1,0:T(1,128)}), f32[64,1,2048]{2,1,0:T(1,128)S(1)}, u32[]{:S(2)}, u32[]{:S(2)}) async-start(f32[64,1,2048]{2,1,0:T(1,128)} %reshape.73), calls=%async_computation | async-start | bytes 1048576 | tf_op jit(solution)/shard_map/while/body/eval_jaxpr/all_to_all | solution.py:50
  562.9 1.0 copy-start.2
  565.5 10.6 %collective-permute-start = (f32[32,512]{0,1:T(8,128)S(1)}, f32[32,512]{0,1:T(8,128)S(1)}, u32[]{:S(2)}, u32[]{:S(2)}) collective-permute-start(f32[32,512]{0,1:T(8,128)S(1)} %scatter_fusion), channel_id=1, source_target_pairs={{0,64},{64,128},{128,192},{192,256},{256,320},{320,384},{384,448},... | collective-permute-start | bytes 196616 | tf_op jit(solution)/shard_map/while/body/eval_jaxpr/ppermute | solution.py:10
  627.2 1.2 copy-start
  631.0 23.1 %all-to-all-start = ((f32[64,1,2048]{2,1,0:T(1,128)}), f32[64,1,2048]{2,1,0:T(1,128)S(1)}, u32[]{:S(2)}, u32[]{:S(2)}) async-start(f32[64,1,2048]{2,1,0:T(1,128)} %reshape.73), calls=%async_computation | async-start | bytes 1048576 | tf_op jit(solution)/shard_map/while/body/eval_jaxpr/all_to_all | solution.py:50
  657.5 1.0 copy-start.2
  660.1 10.6 %collective-permute-start = (f32[32,512]{0,1:T(8,128)S(1)}, f32[32,512]{0,1:T(8,128)S(1)}, u32[]{:S(2)}, u32[]{:S(2)}) collective-permute-start(f32[32,512]{0,1:T(8,128)S(1)} %scatter_fusion), channel_id=1, source_target_pairs={{0,64},{64,128},{128,192},{192,256},{256,320},{320,384},{384,448},... | collective-permute-start | bytes 196616 | tf_op jit(solution)/shard_map/while/body/eval_jaxpr/ppermute | solution.py:10
  670.7 0.7 copy-start.3
  722.5 1.2 copy-start.1
